TPU v7x, 128 devices: a whole 4x4x4 slice. The times are simulated.
128 devices in a mesh: rep: 64 (over z, y, x_hi, core), shard: 2 (over x_lo).
Axes of the slice: x: 4 (x_hi: 2, x_lo: 2; x = x_hi * 2 + x_lo), y: 4, z: 4, core: 2. Of those that a mesh axis runs over, the one named last changes fastest.
Arguments:
- grad_xproj: bfloat16 [256, 2, 3072, 128], P(('rep', 'shard')), may hold values from -32 to 32
- grad_chan: bfloat16 [256, 2, 118, 3072], P(('rep', 'shard')), may hold values from -32 to 32
- grad_embed: bfloat16 [256, 1024, 1536], P(('rep', 'shard')), may hold values from -32 to 32
- weight_xproj: float32 [2, 3072, 128], P(None, 'shard'), may hold values from -0.3125 to 0.3125
- weight_chan: float32 [2, 118, 3072], P(None, None, 'shard'), may hold values from -0.3125 to 0.3125
- weight_embed: float32 [1024, 1536], P('shard'), may hold values from -0.3125 to 0.3125
- moment_xproj: float32 [2, 3072, 128], P(None, 'shard'), may hold values from -0.015625 to 0.015625
- moment_chan: float32 [2, 118, 3072], P(None, None, 'shard'), may hold values from -0.015625 to 0.015625
- moment_embed: float32 [1024, 1536], P('shard'), may hold values from -0.015625 to 0.015625
- second_xproj: float32 [2, 3072, 128], P(None, 'shard'), may hold values from 1e-08 to 1e-05
- second_chan: float32 [2, 118, 3072], P(None, None, 'shard'), may hold values from 1e-08 to 1e-05
- second_embed: float32 [1024, 1536], P('shard'), may hold values from 1e-08 to 1e-05
Outputs:
- new_weight_xproj: float32 [2, 3072, 128], P(None, 'shard')
- new_weight_chan: float32 [2, 118, 3072], P(None, None, 'shard')
- new_weight_embed: float32 [1024, 1536], P('shard')
- new_moment_xproj: float32 [2, 3072, 128], P(None, 'shard')
- new_moment_chan: float32 [2, 118, 3072], P(None, None, 'shard')
- new_moment_embed: float32 [1024, 1536], P('shard')
- new_second_xproj: float32 [2, 3072, 128], P(None, 'shard')
- new_second_chan: float32 [2, 118, 3072], P(None, None, 'shard')
- new_second_embed: float32 [1024, 1536], P('shard')
- full_xproj: bfloat16 [2, 3072, 128], replicated
- full_chan: bfloat16 [2, 118, 3072], replicated
- full_embed: bfloat16 [1024, 1536], replicated
- pre_norm: float32 [1], replicated
All inputs are finite; a program needn't handle non-finite values.
Results may differ from a plain program's by a relative error of at most 0.00085.
Values may be sent and summed in bfloat16 or wider, within the bound.
No kernel may reach another device: no remote copies, remote signals or barrier semaphores. Data moves between devices by JAX's collectives and lax.ppermute only.
A program may use at most 448 MiB of HBM per device.

v0:
```python
import jax
import jax.numpy as jnp
from jax import lax
from jax.sharding import Mesh, PartitionSpec as P

beta_one = 0.9
beta_two = 0.999
learn_rate = 0.003
decay_rate = 0.1
epsilon = 1e-08
correct_one = 0.9999734386011124
correct_two = 0.09520785288629094

AXES = ("z", "y", "xh", "core", "shard")
XRING = ("xh", "shard")


def adamw_update(weight, moment, second, gradient, clip_factor):
    clipped = clip_factor * gradient
    new_moment = beta_one * moment + (1.0 - beta_one) * clipped
    new_second = beta_two * second + (1.0 - beta_two) * clipped * clipped
    step_size = new_moment / correct_one / (jnp.sqrt(new_second / correct_two) + epsilon)
    new_weight = weight - learn_rate * (step_size + decay_rate * weight)
    return (new_weight, new_moment, new_second)


def reduce_flat(buf):
    me = lax.axis_index("core")
    flip = [(0, 1), (1, 0)]
    low = [b.astype(jnp.bfloat16) for b in buf]
    to_low = lax.ppermute(low[0], "core", perm=[(1, 0)])
    to_high = lax.ppermute(low[1], "core", perm=[(0, 1)])
    first = me == 0
    mine = jnp.where(first, low[0], low[1])
    got = jnp.where(first, to_low, to_high)
    part = (mine.astype(jnp.float32) + got.astype(jnp.float32)).astype(jnp.bfloat16)
    part = lax.psum_scatter(part, XRING, scatter_dimension=0, tiled=False)
    part = lax.psum_scatter(part, "y", scatter_dimension=0, tiled=False)
    part = lax.psum(part.astype(jnp.float32), "z").astype(jnp.bfloat16)
    wide = part.astype(jnp.float32)
    squares = jnp.sum(wide * wide)
    for axis in ("core", XRING, "y"):
        squares = lax.psum(squares, axis)
    part = lax.all_gather(part, "y", axis=0)
    part = lax.all_gather(part, "xh", axis=0)
    part, squares = lax.optimization_barrier((part, squares))
    other = lax.ppermute(part, "core", perm=flip)
    part = jnp.stack([jnp.where(first, part, other), jnp.where(first, other, part)])
    return part, squares


TR = 16


def to_tiles(a):
    *lead, r, c = a.shape
    a = a.reshape(*lead, r // TR, TR, c // 128, 128)
    n = len(lead)
    return jnp.swapaxes(a, n + 1, n + 2)


def from_tiles(t, r, c):
    *lead, _, _, _, _ = t.shape
    n = len(lead)
    return jnp.swapaxes(t, n + 1, n + 2).reshape(*lead, r, c)


def swap_halves(own, split_axis):
    n = lax.axis_size(XRING)
    first, second = jnp.split(own, 2, axis=split_axis)
    from_left = lax.ppermute(first, XRING, perm=[(p, (p + 1) % n) for p in range(n)])
    from_right = lax.ppermute(second, XRING, perm=[(p, (p - 1) % n) for p in range(n)])
    return jnp.concatenate([from_left, from_right], axis=split_axis)


def place(own, other, axis):
    low = lax.axis_index("shard") == 0
    lo = jnp.where(low, own, other)
    hi = jnp.where(low, other, own)
    return jnp.concatenate([lo, hi], axis=axis)


def on_device(
    grad_xproj,
    grad_chan,
    grad_embed,
    weight_xproj,
    weight_chan,
    weight_embed,
    moment_xproj,
    moment_chan,
    moment_embed,
    second_xproj,
    second_chan,
    second_embed,
):
    n_core = lax.axis_size("core")
    n_xh = lax.axis_size("xh")
    n_y = lax.axis_size("y")
    n_s = lax.axis_size("shard")
    total = grad_xproj.shape[0] * lax.axis_size(AXES)
    layers, inner, xw = grad_xproj.shape[1:]
    ch = grad_chan.shape[2]
    rows_e, width = grad_embed.shape[1:]
    half = inner // n_s

    n_x = n_xh * n_s
    cut = n_core * n_xh * n_y
    sx = to_tiles(jnp.sum(grad_xproj, axis=0, dtype=jnp.float32))
    tx = sx.reshape(layers, n_s, inner // (TR * n_s), TR, 128)
    tx = jnp.transpose(tx, (1, 0, 2, 3, 4)).reshape(n_s, -1, TR, 128)

    ch_pad = -(-ch // TR) * TR
    sc = jnp.sum(grad_chan, axis=0, dtype=jnp.float32)
    sc = to_tiles(jnp.pad(sc, ((0, 0), (0, ch_pad - ch), (0, 0))))
    lanes_c = half // 128
    tc = sc.reshape(layers, ch_pad // TR, n_s, lanes_c, TR, 128)
    tc = jnp.transpose(tc, (2, 0, 1, 3, 4, 5)).reshape(n_s, -1, TR, 128)

    se = to_tiles(jnp.sum(grad_embed, axis=0, dtype=jnp.float32))
    te = se.reshape(n_s, -1, TR, 128)

    counts = (tc.shape[1], tx.shape[1], te.shape[1])
    used = sum(counts)
    per = -(-used // cut)
    fits = per * cut == used and counts[0] == counts[1] and counts[2] == 2 * counts[0] and n_core == n_xh == 2
    if fits:
        lead = [a.reshape(n_s, n_y, per, TR, 128) for a in (tc, tx)]
        rest = jnp.swapaxes(te.reshape(n_s, n_xh, n_y, per, TR, 128), 0, 1)
        buf = [jnp.stack(lead).reshape(n_x, n_y, per, TR, 128), rest.reshape(n_x, n_y, per, TR, 128)]
    else:
        parts = [tc, tx, te]
        if per * cut > used:
            parts.append(jnp.zeros((n_s, per * cut - used, TR, 128), jnp.float32))
        tiles = jnp.concatenate(parts, axis=1)
        buf = tiles.reshape(n_s, n_core, n_xh, n_y, per, TR, 128)
        buf = list(jnp.transpose(buf, (1, 2, 0, 3, 4, 5, 6)).reshape(n_core, n_x, n_y, per, TR, 128))

    summed_t, sum_squares = reduce_flat(buf)
    mean_t = summed_t.reshape(per * cut, TR, 128)
    inverse = 1.0 / total
    mt = mean_t.astype(jnp.float32) * inverse
    gc = mt[: counts[0]].reshape(layers, ch_pad // TR, lanes_c, TR, 128)
    mean_c = from_tiles(gc, ch_pad, half)[:, :ch, :]
    gx = mt[counts[0] : counts[0] + counts[1]].reshape(layers, half // TR, 1, TR, 128)
    mean_x = from_tiles(gx, half, xw)
    ge = mt[counts[0] + counts[1] : used].reshape(rows_e // (TR * n_s), width // 128, TR, 128)
    mean_e = from_tiles(ge, rows_e // n_s, width)

    squares = sum_squares * (inverse * inverse)
    norm_value = jnp.sqrt(squares)
    clip_factor = jnp.minimum(1.0, 1.0 / (norm_value + 1e-06))
    wx, mx, vx = adamw_update(weight_xproj, moment_xproj, second_xproj, mean_x, clip_factor)
    wc, mc, vc = adamw_update(weight_chan, moment_chan, second_chan, mean_c, clip_factor)
    we, me, ve = adamw_update(weight_embed, moment_embed, second_embed, mean_e, clip_factor)
    bx = wx.astype(jnp.bfloat16)
    bc = wc.astype(jnp.bfloat16)
    be = we.astype(jnp.bfloat16)
    full_x = place(bx, swap_halves(bx, 0), 1)
    full_c = place(bc, swap_halves(bc, 0), 2)
    full_e = place(be, swap_halves(be, 0), 0)
    return (wx, wc, we, mx, mc, me, vx, vc, ve, full_x, full_c, full_e, jnp.reshape(norm_value, (1,)))


def solution(mesh):
    rep = mesh.shape["rep"]
    fine = Mesh(mesh.devices.reshape(rep // 16, 4, 2, 2, mesh.shape["shard"]), AXES)
    grads = ("z", "y", "xh", "core", "shard")
    placed = (
        P(grads, None, None, None),
        P(grads, None, None, None),
        P(grads, None, None),
        P(None, "shard", None),
        P(None, None, "shard"),
        P("shard", None),
        P(None, "shard", None),
        P(None, None, "shard"),
        P("shard", None),
        P(None, "shard", None),
        P(None, None, "shard"),
        P("shard", None),
    )
    return jax.shard_map(
        on_device,
        mesh=fine,
        in_specs=placed,
        out_specs=(
            P(None, "shard", None),
            P(None, None, "shard"),
            P("shard", None),
            P(None, "shard", None),
            P(None, None, "shard"),
            P("shard", None),
            P(None, "shard", None),
            P(None, None, "shard"),
            P("shard", None),
            P(),
            P(),
            P(),
            P(),
        ),
        check_vma=False,
    )
```

profile of v0, /device:TPU:0, one launch (start us, length us, event | category | flops | bytes accessed | tf_op | source)
XLA Modules:
  0.0 255.1 jit_solution(8318533380489351333)
XLA Ops:
  7.2 6.5 %reduce = bf16[2,118,3072]{2,0,1:T(2,128)(2,1)S(1)} reduce(bf16[2,2,118,3072]{3,1,2,0:T(2,128)(2,1)} %param.13, bf16[]{:T(256)} %constant.21.clone.1), dimensions={0}, to_apply=%region_0.0.clone | reduce | flops 724992 | bytes 4349954 | tf_op jit(solution)/shard_map/reduce_sum | solution.py:114
  13.7 1.2 pad.5
  14.9 1.0 reshape.77
  16.0 0.4 copy.52
  16.4 0.3 copy.53
  16.7 2.9 %reduce.1 = bf16[2,3072,128]{2,1,0:T(8,128)(2,1)S(1)} reduce(bf16[2,2,3072,128]{3,2,1,0:T(8,128)(2,1)} %param.12, bf16[]{:T(256)} %constant.21.clone.1), dimensions={0}, to_apply=%region_1.0.clone | reduce | flops 786432 | bytes 4718594 | tf_op jit(solution)/shard_map/reduce_sum | solution.py:109
  19.6 0.3 copy.54
  19.9 1.9 pad_maximum_fusion
  21.8 1.5 collective-permute-start
  23.3 6.1 %reduce.2 = bf16[1024,1536]{1,0:T(8,128)(2,1)S(1)} reduce(bf16[2,1024,1536]{2,1,0:T(8,128)(2,1)} %param.14, bf16[]{:T(256)} %constant.21.clone.1), dimensions={0}, to_apply=%region_2.3.clone | reduce | flops 1572864 | bytes 9437186 | tf_op jit(solution)/shard_map/reduce_sum | solution.py:120
  29.4 3.7 %reshape.70 = bf16[64,16,12,128]{3,2,1,0:T(8,128)(2,1)} reshape(bf16[1024,1536]{1,0:T(8,128)(2,1)S(1)} %reduce.2) | data formatting | bytes 6291456 | tf_op jit(solution)/shard_map/reshape | solution.py:57
  33.0 3.0 %copy.55 = bf16[64,12,16,128]{3,2,1,0:T(8,128)(2,1)S(1)} copy(bf16[64,12,16,128]{3,1,2,0:T(8,128)(2,1)} %bitcast.55) | data formatting | bytes 6291456 | tf_op jit(solution)/shard_map/convert_element_type | solution.py:30
  36.0 0.5 copy.56
  36.6 6.2 %collective-permute-start.1 = (bf16[4,4,48,16,128]{4,3,2,1,0:T(8,128)(2,1)S(1)}, bf16[4,4,48,16,128]{4,3,2,1,0:T(8,128)(2,1)}, u32[]{:S(2)}, u32[]{:S(2)}) collective-permute-start(bf16[4,4,48,16,128]{4,3,2,1,0:T(8,128)(2,1)S(1)} %bitcast.59), channel_id=1, source_target_pairs={{0,2},{1,3},{4,6},{5,7},{8,10},{9,11},{12,14},{13,15},{16,18},{17,... | collective-permute-start | bytes 9437192 | tf_op jit(solution)/shard_map/ppermute | solution.py:32
  42.8 3.7 %collective-permute-done.1 = bf16[4,4,48,16,128]{4,3,2,1,0:T(8,128)(2,1)} collective-permute-done((bf16[4,4,48,16,128]{4,3,2,1,0:T(8,128)(2,1)S(1)}, bf16[4,4,48,16,128]{4,3,2,1,0:T(8,128)(2,1)}, u32[]{:S(2)}, u32[]{:S(2)}) %collective-permute-start.1) | collective-permute-done | bytes 3145760 | tf_op jit(solution)/shard_map/ppermute | solution.py:32
  46.5 6.7 %add_convert_fusion = bf16[4,4,48,16,128]{4,3,2,1,0:T(8,128)(2,1)} fusion(bf16[4,4,48,16,128]{4,3,2,1,0:T(8,128)(2,1)} %collective-permute-done, bf16[4,4,48,16,128]{4,3,2,1,0:T(8,128)(2,1)} %collective-permute-done.1, pred[]{:T(512)S(6)} %eq.8, bf16[2,2,4,48,16,128]{5,4,3,2,1,0:T(8,128)(2,1)S(1)} %copy.56, bf16[2,2,4,48,16,128]{5,4,3,2,1,0:T(8,128)(2,1)} %pad_maximum_fusion), kind=kLoop, calls=%fused_computation.1 | loop fusion | flops 9437184 | bytes 15728641 | tf_op jit(solution)/shard_map/convert_element_type | solution.py:36
  53.2 0.0 reduce-scatter.5.cloned.1.call-start
  53.3 40.8 %reduce-scatter.3.cloned.1.call-done = bf16[1,4,48,16,128]{4,3,2,1,0:T(8,128)(2,1)} async-done(((bf16[4,4,48,16,128]{4,3,2,1,0:T(8,128)(2,1)}), bf16[1,4,48,16,128]{4,3,2,1,0:T(8,128)(2,1)}) %reduce-scatter.3.cloned.1.call-update) | async-done | bytes 786448 | tf_op jit(solution)/shard_map/reduce_scatter | solution.py:37
  94.2 24.6 %reduce-scatter.5.cloned.1.call-done = bf16[1,48,16,128]{3,2,1,0:T(8,128)(2,1)} async-done(((bf16[4,48,16,128]{3,2,1,0:T(8,128)(2,1)}), bf16[1,48,16,128]{3,2,1,0:T(8,128)(2,1)}) %reduce-scatter.5.cloned.1.call-update) | async-done | bytes 196624 | tf_op jit(solution)/shard_map/reduce_scatter | solution.py:38
  118.8 1.0 bitcast_convert_fusion
  119.8 21.0 %all-reduce.2 = bf16[48,16,128]{2,1,0:T(8,128)(2,1)S(1)} all-reduce(f32[48,16,128]{2,1,0:T(8,128)S(1)} %bitcast_convert_fusion), channel_id=1, replica_groups=mesh['z'=4,'y'=4,'xh'=2,'core'=2,'shard'=2] {'z'}, use_global_device_ids=true, to_apply=%region_5.6 | all-reduce | flops 98304 | bytes 589824 | tf_op jit(solution)/shard_map/psum | solution.py:39
  140.8 15.1 %all-gather = bf16[192,16,128]{2,1,0:T(8,128)(2,1)} all-gather(bf16[48,16,128]{2,1,0:T(8,128)(2,1)S(1)} %all-reduce.2), channel_id=2, replica_groups=mesh['z'=4,'y'=4,'xh'=2,'core'=2,'shard'=2] {'y'}, dimensions={0}, use_global_device_ids=true | all-gather | bytes 983040 | tf_op jit(solution)/shard_map/all_gather | solution.py:44
  155.9 0.7 multiply_reduce_fusion
  156.6 3.1 %psum.29 = f32[]{:T(128)} all-reduce(f32[]{:T(128)} %multiply_reduce_fusion), channel_id=1, replica_groups=mesh['z'=4,'y'=4,'xh'=2,'core'=2,'shard'=2] {'core'}, use_global_device_ids=true, to_apply=%region_7.8 | all-reduce | flops 1 | bytes 8 | tf_op jit(solution)/shard_map/psum | solution.py:43
  159.7 11.4 %psum.30 = f32[]{:T(128)} all-reduce(f32[]{:T(128)} %psum.29), channel_id=1, replica_groups=mesh['z'=4,'y'=4,'xh'=2,'core'=2,'shard'=2] {'xh','shard'}, use_global_device_ids=true, to_apply=%region_8.9 | all-reduce | flops 1 | bytes 8 | tf_op jit(solution)/shard_map/psum | solution.py:43
  171.1 8.5 %psum.31 = f32[]{:T(128)} all-reduce(f32[]{:T(128)} %psum.30), channel_id=1, replica_groups=mesh['z'=4,'y'=4,'xh'=2,'core'=2,'shard'=2] {'y'}, use_global_device_ids=true, to_apply=%region_9.10 | all-reduce | flops 1 | bytes 8 | tf_op jit(solution)/shard_map/psum | solution.py:43
  179.6 5.9 %all-gather.4.cloned.1.call-done = bf16[8,48,16,128]{3,2,1,0:T(8,128)(2,1)} async-done(((bf16[4,48,16,128]{3,2,1,0:T(8,128)(2,1)}), bf16[8,48,16,128]{3,2,1,0:T(8,128)(2,1)}) %all-gather.4.cloned.1.call-update) | async-done | bytes 1572880 | tf_op jit(solution)/shard_map/all_gather | solution.py:45
  186.2 2.9 %collective-permute-done.2 = bf16[2,4,48,16,128]{4,3,2,1,0:T(8,128)(2,1)S(1)} collective-permute-done((bf16[2,4,48,16,128]{4,3,2,1,0:T(8,128)(2,1)}, bf16[2,4,48,16,128]{4,3,2,1,0:T(8,128)(2,1)S(1)}, u32[]{:S(2)}, u32[]{:S(2)}) %collective-permute-start.2) | collective-permute-done | bytes 1572896 | tf_op jit(solution)/shard_map/ppermute | solution.py:47
  189.1 1.6 select_bitcast_fusion.1
  190.7 0.6 convert_multiply_fusion
  191.3 0.2 slice_multiply_fusion
  191.6 1.3 copy.62
  192.9 0.3 copy-done.2
  193.2 1.0 copy-done
  194.2 0.9 copy-done.1
  195.2 5.6 %fusion.6 = (bf16[512,1536]{1,0:T(8,128)(2,1)S(1)}, f32[512,1536]{1,0:T(8,128)}, f32[512,1536]{1,0:T(8,128)}, f32[512,1536]{1,0:T(8,128)}) fusion(f32[512,1536]{1,0:T(8,128)S(1)} %copy-done, f32[64,8,12,128]{3,2,1,0:T(8,128)S(1)} %bitcast.56, f32[512,1536]{1,0:T(8,128)S(1)} %copy-done.1, f32[512,1536]{1,0:T(8,128)S(1)} %copy-done.2), kind=kLoop, calls=%fused_computation.41 | loop fusion | flops 12582912 | bytes 23592960 | tf_op jit(solution)/shard_map/convert_element_type | solution.py:158
  200.7 1.3 fusion.16
  202.0 0.5 collective-permute-start.7
  202.5 2.8 %collective-permute-start.8 = (bf16[256,1536]{1,0:T(8,128)(2,1)}, bf16[256,1536]{1,0:T(8,128)(2,1)}, u32[]{:S(2)}, u32[]{:S(2)}) collective-permute-start(bf16[256,1536]{1,0:T(8,128)(2,1)} %get-tuple-element.74), channel_id=1, source_target_pairs={{0,5},{1,0},{4,1},{5,4},{2,7},{3,2},{6,3},{7,6},{8,13},{9,8},{12,9... | collective-permute-start | bytes 2359304 | tf_op jit(solution)/shard_map/ppermute | solution.py:72
  205.2 0.2 fusion.15
  205.4 1.8 copy.58
  207.3 2.6 %reshape.72 = f32[2,128,1536]{2,1,0:T(8,128)} reshape(f32[2,8,16,12,128]{4,3,2,1,0:T(8,128)} %copy.58) | data formatting | bytes 3145728 | tf_op jit(solution)/shard_map/reshape | solution.py:65
  209.9 4.3 %fusion.9 = (bf16[2,118,1536]{2,1,0:T(8,128)(2,1)S(1)}, f32[2,118,1536]{2,1,0:T(8,128)S(1)}, f32[2,118,1536]{2,1,0:T(8,128)S(1)}, f32[2,118,1536]{2,1,0:T(8,128)S(1)}) fusion(f32[2,118,1536]{2,0,1:T(2,128)} %param.16, f32[2,128,1536]{2,1,0:T(8,128)} %reshape.72, f32[]{:T(128)S(6)} %min.3, f32[2,118,1536]{2,0,1:T(2,128)} %param.19, f32[2,118,1536]{2,0,1:T(2,128)} %param.22), kind=kLoop, calls=%fused_computation.42 | loop fusion | flops 6162432 | bytes 10874884 | tf_op jit(solution)/shard_map/convert_element_type | solution.py:157
  214.2 0.1 collective-permute-start.5
  214.3 3.2 %collective-permute-start.6 = (bf16[1,118,1536]{2,1,0:T(8,128)(2,1)S(1)}, bf16[1,118,1536]{2,1,0:T(8,128)(2,1)S(1)}, u32[]{:S(2)}, u32[]{:S(2)}) collective-permute-start(bf16[1,118,1536]{2,1,0:T(8,128)(2,1)S(1)} %get-tuple-element.82), channel_id=1, source_target_pairs={{0,5},{1,0},{4,1},{5,4},{2,7},{3,2},{6,3},{7,6},{8,13},{9,8},{12,9... | collective-permute-start | bytes 1087496 | tf_op jit(solution)/shard_map/ppermute | solution.py:72
  217.5 3.0 %fusion.12 = (bf16[2,1536,128]{2,1,0:T(8,128)(2,1)S(1)}, f32[2,1536,128]{2,1,0:T(8,128)}, f32[2,1536,128]{2,1,0:T(8,128)}, f32[2,1536,128]{2,1,0:T(8,128)}) fusion(f32[2,1536,128]{2,1,0:T(8,128)S(1)} %copy-done.3, f32[2,1536,128]{2,1,0:T(8,128)S(1)} %copy-done.4, f32[2,1536,128]{2,1,0:T(8,128)S(1)} %copy-done.5, f32[2,1536,128]{2,1,0:T(8,128)S(1)} %bitcast.66), kind=kLoop, calls=%fused_computation.43 | loop fusion | flops 6291456 | bytes 11796480 | tf_op jit(solution)/shard_map/convert_element_type | solution.py:156
  220.5 0.1 fusion.17
  220.6 0.3 collective-permute-start.3
  220.9 2.2 copy.63
  223.2 2.2 copy.64
  225.4 2.2 copy.65
  227.6 4.1 %collective-permute-done.5 = bf16[1,118,1536]{2,1,0:T(8,128)(2,1)S(1)} collective-permute-done((bf16[1,118,1536]{2,1,0:T(8,128)(2,1)S(1)}, bf16[1,118,1536]{2,1,0:T(8,128)(2,1)S(1)}, u32[]{:S(2)}, u32[]{:S(2)}) %collective-permute-start.5) | collective-permute-done | bytes 362528 | tf_op jit(solution)/shard_map/ppermute | solution.py:71
  231.8 0.1 broadcast_select_fusion.5
  231.9 0.2 pad_maximum_fusion.3
  232.1 2.6 %copy.66 = bf16[2,118,3072]{2,0,1:T(2,128)(2,1)} copy(bf16[2,118,3072]{2,1,0:T(8,128)(2,1)S(1)} %pad_maximum_fusion.3) | data formatting | bytes 2899968
  234.7 4.7 %collective-permute-done.3 = bf16[1,1536,128]{2,1,0:T(8,128)(2,1)S(1)} collective-permute-done((bf16[1,1536,128]{2,1,0:T(8,128)(2,1)S(1)}, bf16[1,1536,128]{2,1,0:T(8,128)(2,1)S(1)}, u32[]{:S(2)}, u32[]{:S(2)}) %collective-permute-start.3) | collective-permute-done | bytes 393248 | tf_op jit(solution)/shard_map/ppermute | solution.py:71
  239.4 1.9 collective-permute-done.4
  241.2 0.1 constant_dynamic-update-slice_fusion
  241.3 0.2 broadcast_select_fusion.3
  241.5 1.2 pad_maximum_fusion.2
  242.7 1.2 constant_dynamic-update-slice_fusion.5
  243.9 1.2 constant_dynamic-update-slice_fusion.4
  245.1 0.4 broadcast_select_fusion.1
  245.5 1.9 pad_maximum_fusion.1
  (24 shorter events, 0.3 us)
Async XLA Ops:
  7.2 86.9 %reduce-scatter.3.cloned.1.call-start = ((), (), s32[]{:S(2)}) async-start(), calls=%async_computation.2 | async-start | bytes 3932160 | tf_op jit(solution)/shard_map/reduce_scatter | solution.py:37
  21.8 20.9 %collective-permute-start = (bf16[4,4,48,16,128]{4,3,2,1,0:T(8,128)(2,1)}, bf16[4,4,48,16,128]{4,3,2,1,0:T(8,128)(2,1)}, u32[]{:S(2)}, u32[]{:S(2)}) collective-permute-start(bf16[4,4,48,16,128]{4,3,2,1,0:T(8,128)(2,1)} %bitcast.8), channel_id=1, source_target_pairs={{2,0},{3,1},{6,4},{7,5},{10,8},{11,9},{14,12},{15,13},{18,16},{19,... | collective-permute-start | bytes 9437192 | tf_op jit(solution)/shard_map/ppermute | solution.py:31
  36.6 9.9 %collective-permute-start.1 = (bf16[4,4,48,16,128]{4,3,2,1,0:T(8,128)(2,1)S(1)}, bf16[4,4,48,16,128]{4,3,2,1,0:T(8,128)(2,1)}, u32[]{:S(2)}, u32[]{:S(2)}) collective-permute-start(bf16[4,4,48,16,128]{4,3,2,1,0:T(8,128)(2,1)S(1)} %bitcast.59), channel_id=1, source_target_pairs={{0,2},{1,3},{4,6},{5,7},{8,10},{9,11},{12,14},{13,15},{16,18},{17,... | collective-permute-start | bytes 9437192 | tf_op jit(solution)/shard_map/ppermute | solution.py:32
  53.2 65.6 %reduce-scatter.5.cloned.1.call-start = ((), (), s32[]{:S(2)}) async-start(), calls=%async_computation.3 | async-start | bytes 983040 | tf_op jit(solution)/shard_map/reduce_scatter | solution.py:38
  94.1 91.3 %all-gather.4.cloned.1.call-start = ((), (), s32[]{:S(2)}) async-start(), calls=%async_computation.4 | async-start | bytes 2359296 | tf_op jit(solution)/shard_map/all_gather | solution.py:45
  185.5 3.6 %collective-permute-start.2 = (bf16[2,4,48,16,128]{4,3,2,1,0:T(8,128)(2,1)}, bf16[2,4,48,16,128]{4,3,2,1,0:T(8,128)(2,1)S(1)}, u32[]{:S(2)}, u32[]{:S(2)}) collective-permute-start(bf16[2,4,48,16,128]{4,3,2,1,0:T(8,128)(2,1)} %bitcast.68), channel_id=1, source_target_pairs={{0,2},{2,0},{1,3},{3,1},{4,6},{6,4},{5,7},{7,5},{8,10},{10,8},{9,1... | collective-permute-start | bytes 4718600 | tf_op jit(solution)/shard_map/ppermute | solution.py:47
  191.3 1.9 copy-start.2
  191.6 2.7 %copy-start = (f32[512,1536]{1,0:T(8,128)S(1)}, f32[512,1536]{1,0:T(8,128)}, u32[]{:S(2)}) copy-start(f32[512,1536]{1,0:T(8,128)} %param.17) | copy-start | bytes 9437188
  191.6 3.6 %copy-start.1 = (f32[512,1536]{1,0:T(8,128)S(1)}, f32[512,1536]{1,0:T(8,128)}, u32[]{:S(2)}) copy-start(f32[512,1536]{1,0:T(8,128)} %param.20) | copy-start | bytes 9437188
  202.0 40.7 %collective-permute-start.7 = (bf16[256,1536]{1,0:T(8,128)(2,1)}, bf16[256,1536]{1,0:T(8,128)(2,1)}, u32[]{:S(2)}, u32[]{:S(2)}) collective-permute-start(bf16[256,1536]{1,0:T(8,128)(2,1)} %get-tuple-element.75), channel_id=1, source_target_pairs={{0,1},{1,4},{4,5},{5,0},{2,3},{3,6},{6,7},{7,2},{8,9},{9,12},{12,1... | collective-permute-start | bytes 2359304 | tf_op jit(solution)/shard_map/ppermute | solution.py:71
  202.5 41.4 %collective-permute-start.8 = (bf16[256,1536]{1,0:T(8,128)(2,1)}, bf16[256,1536]{1,0:T(8,128)(2,1)}, u32[]{:S(2)}, u32[]{:S(2)}) collective-permute-start(bf16[256,1536]{1,0:T(8,128)(2,1)} %get-tuple-element.74), channel_id=1, source_target_pairs={{0,5},{1,0},{4,1},{5,4},{2,7},{3,2},{6,3},{7,6},{8,13},{9,8},{12,9... | collective-permute-start | bytes 2359304 | tf_op jit(solution)/shard_map/ppermute | solution.py:72
  209.9 7.7 %copy-start.3 = (f32[2,1536,128]{2,1,0:T(8,128)S(1)}, f32[2,1536,128]{2,1,0:T(8,128)}, u32[]{:S(2)}) copy-start(f32[2,1536,128]{2,1,0:T(8,128)} %param.15) | copy-start | bytes 4718596
  209.9 7.7 %copy-start.4 = (f32[2,1536,128]{2,1,0:T(8,128)S(1)}, f32[2,1536,128]{2,1,0:T(8,128)}, u32[]{:S(2)}) copy-start(f32[2,1536,128]{2,1,0:T(8,128)} %param.18) | copy-start | bytes 4718596
  209.9 7.7 %copy-start.5 = (f32[2,1536,128]{2,1,0:T(8,128)S(1)}, f32[2,1536,128]{2,1,0:T(8,128)}, u32[]{:S(2)}) copy-start(f32[2,1536,128]{2,1,0:T(8,128)} %param.21) | copy-start | bytes 4718596
  214.2 17.5 %collective-permute-start.5 = (bf16[1,118,1536]{2,1,0:T(8,128)(2,1)S(1)}, bf16[1,118,1536]{2,1,0:T(8,128)(2,1)S(1)}, u32[]{:S(2)}, u32[]{:S(2)}) collective-permute-start(bf16[1,118,1536]{2,1,0:T(8,128)(2,1)S(1)} %get-tuple-element.83), channel_id=1, source_target_pairs={{0,1},{1,4},{4,5},{5,0},{2,3},{3,6},{6,7},{7,2},{8,9},{9,12},{12,1... | collective-permute-start | bytes 1087496 | tf_op jit(solution)/shard_map/ppermute | solution.py:71
  214.3 17.4 %collective-permute-start.6 = (bf16[1,118,1536]{2,1,0:T(8,128)(2,1)S(1)}, bf16[1,118,1536]{2,1,0:T(8,128)(2,1)S(1)}, u32[]{:S(2)}, u32[]{:S(2)}) collective-permute-start(bf16[1,118,1536]{2,1,0:T(8,128)(2,1)S(1)} %get-tuple-element.82), channel_id=1, source_target_pairs={{0,5},{1,0},{4,1},{5,4},{2,7},{3,2},{6,3},{7,6},{8,13},{9,8},{12,9... | collective-permute-start | bytes 1087496 | tf_op jit(solution)/shard_map/ppermute | solution.py:72
  220.6 18.7 %collective-permute-start.3 = (bf16[1,1536,128]{2,1,0:T(8,128)(2,1)S(1)}, bf16[1,1536,128]{2,1,0:T(8,128)(2,1)S(1)}, u32[]{:S(2)}, u32[]{:S(2)}) collective-permute-start(bf16[1,1536,128]{2,1,0:T(8,128)(2,1)S(1)} %get-tuple-element.81), channel_id=1, source_target_pairs={{0,1},{1,4},{4,5},{5,0},{2,3},{3,6},{6,7},{7,2},{8,9},{9,12},{12,1... | collective-permute-start | bytes 1179656 | tf_op jit(solution)/shard_map/ppermute | solution.py:71
  231.7 9.5 %collective-permute-start.4 = (bf16[1,1536,128]{2,1,0:T(8,128)(2,1)S(1)}, bf16[1,1536,128]{2,1,0:T(8,128)(2,1)S(1)}, u32[]{:S(2)}, u32[]{:S(2)}) collective-permute-start(bf16[1,1536,128]{2,1,0:T(8,128)(2,1)S(1)} %get-tuple-element.80), channel_id=1, source_target_pairs={{0,5},{1,0},{4,1},{5,4},{2,7},{3,2},{6,3},{7,6},{8,13},{9,8},{12,9... | collective-permute-start | bytes 1179656 | tf_op jit(solution)/shard_map/ppermute | solution.py:72
Sparse Core Ops, SparseCore 0:
  53.4 40.6 reduce-scatter.2
  96.5 22.2 reduce-scatter.4
  156.1 29.3 all-gather.3
where the time goes:
time: 256 us; the launch traced here: 255 us
  waiting for transfers between devices  88.6 us (35%)
  blocking collectives  59.1 us (23%)
  other arithmetic  45.4 us (18%)
  local copies, waits for them, and re-layouts  31.5 us (12%)
  between operations  15.9 us (6%)
  starting transfers between devices  14.6 us (6%)
    reduce_scatter x1, waiting for transfers between devices, reduce_flat(): part = lax.psum_scatter(part, XRING, scatter_dimension=0, tiled=False)  40.8 us
    reduce_scatter x1, waiting for transfers between devices, reduce_flat(): part = lax.psum_scatter(part, 'y', scatter_dimension=0, tiled=False)  24.6 us
    psum x3, blocking collectives, reduce_flat(): squares = lax.psum(squares, axis)  22.9 us
    psum x1, blocking collectives, reduce_flat(): part = lax.psum(part.astype(jnp.float32), 'z').astype(jnp.bfloat16)  21 us
    all_gather x1, blocking collectives, reduce_flat(): part = lax.all_gather(part, 'y', axis=0)  15.1 us
    unnamed x19, local copies, waits for them, and re-layouts  12.8 us
    ppermute x3, waiting for transfers between devices, swap_halves(): lax.ppermute(first, XRING, perm=[(p, (p + 1) % n) for p in range(n)])  8.75 us
    convert_element_type x1, other arithmetic, reduce_flat(): (mine.astype(jnp.float32) + got.astype(jnp.float32)).astype(jnp.bfloat16)  6.71 us
  transfers between devices with their start and end apart: 12, of which 8 were waited for; matrix products, arithmetic and copies ran while one was open for 15% of the time, Pallas kernels for 0%

commit v1 on v0

--- a/solution.py
+++ b/solution.py
@@ -36,7 +36,13 @@
     part = (mine.astype(jnp.float32) + got.astype(jnp.float32)).astype(jnp.bfloat16)
     part = lax.psum_scatter(part, XRING, scatter_dimension=0, tiled=False)
     part = lax.psum_scatter(part, "y", scatter_dimension=0, tiled=False)
-    part = lax.psum(part.astype(jnp.float32), "z").astype(jnp.bfloat16)
+    part = part.astype(jnp.float32)
+    n_z = lax.axis_size("z")
+    hop = 1
+    while hop < n_z:
+        part = part + lax.ppermute(part, "z", perm=[(i, i ^ hop) for i in range(n_z)])
+        hop *= 2
+    part = part.astype(jnp.bfloat16)
     wide = part.astype(jnp.float32)
     squares = jnp.sum(wide * wide)
     for axis in ("core", XRING, "y"):

time: 256 us -> 257 us (level)
  blocking collectives: 59.1 us -> 38.1 us
  waiting for transfers between devices: 88.6 us -> 105 us
  starting transfers between devices: 14.6 us -> 19.5 us
    psum x1 -> x0, blocking collectives: 21 us -> none  [reduce_flat(): part = lax.psum(part.astype(jnp.float32), 'z').astype(jnp.bfloat16)]
    ppermute x0 -> x2, waiting for transfers between devices: none -> 15.4 us  [reduce_flat(): lax.ppermute(part, 'z', perm=[(i, i ^ hop) for i in range(n_z)])]
    ppermute x0 -> x2, starting transfers between devices: none -> 4.86 us  [reduce_flat(): lax.ppermute(part, 'z', perm=[(i, i ^ hop) for i in range(n_z)])]
  transfers between devices with their start and end apart: 12 -> 14, of which waited for: 8 -> 10; matrix products, arithmetic and copies ran while one was open for 15% -> 15% of each run, Pallas kernels for 0% -> 0%
where the time goes in v1:
time: 257 us
  waiting for transfers between devices  105 us (41%)
  other arithmetic  46.3 us (18%)
  blocking collectives  38.1 us (15%)
  local copies, waits for them, and re-layouts  31.5 us (12%)
  starting transfers between devices  19.5 us (8%)
  between operations  15.9 us (6%)
    reduce_scatter x1, waiting for transfers between devices, reduce_flat(): part = lax.psum_scatter(part, XRING, scatter_dimension=0, tiled=False)  40.8 us
    reduce_scatter x1, waiting for transfers between devices, reduce_flat(): part = lax.psum_scatter(part, 'y', scatter_dimension=0, tiled=False)  24.6 us
    psum x3, blocking collectives, reduce_flat(): squares = lax.psum(squares, axis)  24.1 us
    ppermute x2, waiting for transfers between devices, reduce_flat(): lax.ppermute(part, 'z', perm=[(i, i ^ hop) for i in range(n_z)])  15.4 us
    all_gather x1, blocking collectives, reduce_flat(): part = lax.all_gather(part, 'y', axis=0)  14 us
    unnamed x19, local copies, waits for them, and re-layouts  12.8 us
    ppermute x3, waiting for transfers between devices, swap_halves(): lax.ppermute(first, XRING, perm=[(p, (p + 1) % n) for p in range(n)])  8.75 us
    all_gather x1, waiting for transfers between devices, reduce_flat(): part = lax.all_gather(part, 'xh', axis=0)  7.09 us
  transfers between devices with their start and end apart: 14, of which 10 were waited for; matrix products, arithmetic and copies ran while one was open for 15% of the time, Pallas kernels for 0%

profile of v1, /device:TPU:0, one launch (start us, length us, event | category | flops | bytes accessed | tf_op | source)
XLA Modules:
  0.0 256.5 jit_solution(18387886624687652651)
XLA Ops:
  7.2 6.5 %reduce = bf16[2,118,3072]{2,0,1:T(2,128)(2,1)S(1)} reduce(bf16[2,2,118,3072]{3,1,2,0:T(2,128)(2,1)} %param.13, bf16[]{:T(256)} %constant.21.clone.1), dimensions={0}, to_apply=%region_0.0.clone | reduce | flops 724992 | bytes 4349954 | tf_op jit(solution)/shard_map/reduce_sum | solution.py:120
  13.7 1.2 pad.5
  14.9 1.0 reshape.77
  16.0 0.4 copy.52
  16.4 0.3 copy.53
  16.7 2.9 %reduce.1 = bf16[2,3072,128]{2,1,0:T(8,128)(2,1)S(1)} reduce(bf16[2,2,3072,128]{3,2,1,0:T(8,128)(2,1)} %param.12, bf16[]{:T(256)} %constant.21.clone.1), dimensions={0}, to_apply=%region_1.0.clone | reduce | flops 786432 | bytes 4718594 | tf_op jit(solution)/shard_map/reduce_sum | solution.py:115
  19.6 0.3 copy.54
  19.9 1.9 pad_maximum_fusion
  21.8 1.5 collective-permute-start
  23.3 6.1 %reduce.2 = bf16[1024,1536]{1,0:T(8,128)(2,1)S(1)} reduce(bf16[2,1024,1536]{2,1,0:T(8,128)(2,1)} %param.14, bf16[]{:T(256)} %constant.21.clone.1), dimensions={0}, to_apply=%region_2.3.clone | reduce | flops 1572864 | bytes 9437186 | tf_op jit(solution)/shard_map/reduce_sum | solution.py:126
  29.4 3.7 %reshape.70 = bf16[64,16,12,128]{3,2,1,0:T(8,128)(2,1)} reshape(bf16[1024,1536]{1,0:T(8,128)(2,1)S(1)} %reduce.2) | data formatting | bytes 6291456 | tf_op jit(solution)/shard_map/reshape | solution.py:63
  33.0 3.0 %copy.55 = bf16[64,12,16,128]{3,2,1,0:T(8,128)(2,1)S(1)} copy(bf16[64,12,16,128]{3,1,2,0:T(8,128)(2,1)} %bitcast.57) | data formatting | bytes 6291456 | tf_op jit(solution)/shard_map/convert_element_type | solution.py:30
  36.0 0.5 copy.56
  36.6 6.2 %collective-permute-start.1 = (bf16[4,4,48,16,128]{4,3,2,1,0:T(8,128)(2,1)S(1)}, bf16[4,4,48,16,128]{4,3,2,1,0:T(8,128)(2,1)}, u32[]{:S(2)}, u32[]{:S(2)}) collective-permute-start(bf16[4,4,48,16,128]{4,3,2,1,0:T(8,128)(2,1)S(1)} %bitcast.61), channel_id=1, source_target_pairs={{0,2},{1,3},{4,6},{5,7},{8,10},{9,11},{12,14},{13,15},{16,18},{17,... | collective-permute-start | bytes 9437192 | tf_op jit(solution)/shard_map/ppermute | solution.py:32
  42.7 3.8 %collective-permute-done.1 = bf16[4,4,48,16,128]{4,3,2,1,0:T(8,128)(2,1)} collective-permute-done((bf16[4,4,48,16,128]{4,3,2,1,0:T(8,128)(2,1)S(1)}, bf16[4,4,48,16,128]{4,3,2,1,0:T(8,128)(2,1)}, u32[]{:S(2)}, u32[]{:S(2)}) %collective-permute-start.1) | collective-permute-done | bytes 3145760 | tf_op jit(solution)/shard_map/ppermute | solution.py:32
  46.5 6.7 %add_convert_fusion = bf16[4,4,48,16,128]{4,3,2,1,0:T(8,128)(2,1)} fusion(bf16[4,4,48,16,128]{4,3,2,1,0:T(8,128)(2,1)} %collective-permute-done, bf16[4,4,48,16,128]{4,3,2,1,0:T(8,128)(2,1)} %collective-permute-done.1, pred[]{:T(512)S(6)} %eq.8, bf16[2,2,4,48,16,128]{5,4,3,2,1,0:T(8,128)(2,1)S(1)} %copy.56, bf16[2,2,4,48,16,128]{5,4,3,2,1,0:T(8,128)(2,1)} %pad_maximum_fusion), kind=kLoop, calls=%fused_computation.1 | loop fusion | flops 9437184 | bytes 15728641 | tf_op jit(solution)/shard_map/convert_element_type | solution.py:36
  53.3 40.8 %reduce-scatter.3.cloned.1.call-done = bf16[1,4,48,16,128]{4,3,2,1,0:T(8,128)(2,1)} async-done(((bf16[4,4,48,16,128]{4,3,2,1,0:T(8,128)(2,1)}), bf16[1,4,48,16,128]{4,3,2,1,0:T(8,128)(2,1)}) %reduce-scatter.3.cloned.1.call-update) | async-done | bytes 786448 | tf_op jit(solution)/shard_map/reduce_scatter | solution.py:37
  94.2 24.6 %reduce-scatter.5.cloned.1.call-done = bf16[1,48,16,128]{3,2,1,0:T(8,128)(2,1)} async-done(((bf16[4,48,16,128]{3,2,1,0:T(8,128)(2,1)}), bf16[1,48,16,128]{3,2,1,0:T(8,128)(2,1)}) %reduce-scatter.5.cloned.1.call-update) | async-done | bytes 196624 | tf_op jit(solution)/shard_map/reduce_scatter | solution.py:38
  118.8 1.0 bitcast_convert_fusion
  119.8 1.6 collective-permute-start.2
  121.4 8.2 %collective-permute-done.2 = f32[48,16,128]{2,1,0:T(8,128)S(1)} collective-permute-done((f32[48,16,128]{2,1,0:T(8,128)S(1)}, f32[48,16,128]{2,1,0:T(8,128)S(1)}, u32[]{:S(2)}, u32[]{:S(2)}) %collective-permute-start.2) | collective-permute-done | bytes 393248 | tf_op jit(solution)/shard_map/ppermute | solution.py:43
  129.6 1.0 fusion.6
  130.6 3.2 %collective-permute-start.3 = (f32[48,16,128]{2,1,0:T(8,128)S(1)}, f32[48,16,128]{2,1,0:T(8,128)S(1)}, u32[]{:S(2)}, u32[]{:S(2)}) collective-permute-start(f32[48,16,128]{2,1,0:T(8,128)S(1)} %fusion.6), channel_id=1, source_target_pairs={{0,64},{32,96},{64,0},{96,32},{1,65},{33,97},{65,1},{97,33},{2,66}... | collective-permute-start | bytes 1179656 | tf_op jit(solution)/shard_map/ppermute | solution.py:43
  133.8 7.2 %collective-permute-done.3 = f32[48,16,128]{2,1,0:T(8,128)S(1)} collective-permute-done((f32[48,16,128]{2,1,0:T(8,128)S(1)}, f32[48,16,128]{2,1,0:T(8,128)S(1)}, u32[]{:S(2)}, u32[]{:S(2)}) %collective-permute-start.3) | collective-permute-done | bytes 393248 | tf_op jit(solution)/shard_map/ppermute | solution.py:43
  141.0 0.7 multiply_reduce_fusion
  141.7 14.0 %all-gather = bf16[192,16,128]{2,1,0:T(8,128)(2,1)} all-gather(bf16[48,16,128]{2,1,0:T(8,128)(2,1)S(1)} %get-tuple-element.69), channel_id=2, replica_groups=mesh['z'=4,'y'=4,'xh'=2,'core'=2,'shard'=2] {'y'}, dimensions={0}, use_global_device_ids=true | all-gather | bytes 983040 | tf_op jit(solution)/shard_map/all_gather | solution.py:50
  155.7 3.1 %psum.21 = f32[]{:T(128)} all-reduce(f32[]{:T(128)} %get-tuple-element.68), channel_id=1, replica_groups=mesh['z'=4,'y'=4,'xh'=2,'core'=2,'shard'=2] {'core'}, use_global_device_ids=true, to_apply=%region_6.7 | all-reduce | flops 1 | bytes 8 | tf_op jit(solution)/shard_map/psum | solution.py:49
  158.8 11.1 %psum.22 = f32[]{:T(128)} all-reduce(f32[]{:T(128)} %psum.21), channel_id=1, replica_groups=mesh['z'=4,'y'=4,'xh'=2,'core'=2,'shard'=2] {'xh','shard'}, use_global_device_ids=true, to_apply=%region_7.8 | all-reduce | flops 1 | bytes 8 | tf_op jit(solution)/shard_map/psum | solution.py:49
  170.0 9.9 %psum.23 = f32[]{:T(128)} all-reduce(f32[]{:T(128)} %psum.22), channel_id=1, replica_groups=mesh['z'=4,'y'=4,'xh'=2,'core'=2,'shard'=2] {'y'}, use_global_device_ids=true, to_apply=%region_8.9 | all-reduce | flops 1 | bytes 8 | tf_op jit(solution)/shard_map/psum | solution.py:49
  179.8 7.1 %all-gather.4.cloned.1.call-done = bf16[8,48,16,128]{3,2,1,0:T(8,128)(2,1)} async-done(((bf16[4,48,16,128]{3,2,1,0:T(8,128)(2,1)}), bf16[8,48,16,128]{3,2,1,0:T(8,128)(2,1)}) %all-gather.4.cloned.1.call-update) | async-done | bytes 1572880 | tf_op jit(solution)/shard_map/all_gather | solution.py:51
  187.7 2.9 %collective-permute-done.4 = bf16[2,4,48,16,128]{4,3,2,1,0:T(8,128)(2,1)S(1)} collective-permute-done((bf16[2,4,48,16,128]{4,3,2,1,0:T(8,128)(2,1)}, bf16[2,4,48,16,128]{4,3,2,1,0:T(8,128)(2,1)S(1)}, u32[]{:S(2)}, u32[]{:S(2)}) %collective-permute-start.4) | collective-permute-done | bytes 1572896 | tf_op jit(solution)/shard_map/ppermute | solution.py:53
  190.5 1.6 select_bitcast_fusion.1
  192.2 0.6 convert_multiply_fusion
  192.8 0.2 slice_multiply_fusion
  193.1 1.3 copy.62
  194.3 0.3 copy-done.2
  194.7 1.0 copy-done
  195.7 0.9 copy-done.1
  196.6 5.6 %fusion.7 = (bf16[512,1536]{1,0:T(8,128)(2,1)S(1)}, f32[512,1536]{1,0:T(8,128)}, f32[512,1536]{1,0:T(8,128)}, f32[512,1536]{1,0:T(8,128)}) fusion(f32[512,1536]{1,0:T(8,128)S(1)} %copy-done, f32[64,8,12,128]{3,2,1,0:T(8,128)S(1)} %bitcast.58, f32[512,1536]{1,0:T(8,128)S(1)} %copy-done.1, f32[512,1536]{1,0:T(8,128)S(1)} %copy-done.2), kind=kLoop, calls=%fused_computation.43 | loop fusion | flops 12582912 | bytes 23592960 | tf_op jit(solution)/shard_map/convert_element_type | solution.py:164
  202.2 1.3 fusion.17
  203.4 0.6 collective-permute-start.9
  204.0 2.7 %collective-permute-start.10 = (bf16[256,1536]{1,0:T(8,128)(2,1)}, bf16[256,1536]{1,0:T(8,128)(2,1)}, u32[]{:S(2)}, u32[]{:S(2)}) collective-permute-start(bf16[256,1536]{1,0:T(8,128)(2,1)} %get-tuple-element.76), channel_id=1, source_target_pairs={{0,5},{1,0},{4,1},{5,4},{2,7},{3,2},{6,3},{7,6},{8,13},{9,8},{12,9... | collective-permute-start | bytes 2359304 | tf_op jit(solution)/shard_map/ppermute | solution.py:78
  206.7 0.2 fusion.16
  206.9 1.8 copy.58
  208.7 2.6 %reshape.72 = f32[2,128,1536]{2,1,0:T(8,128)} reshape(f32[2,8,16,12,128]{4,3,2,1,0:T(8,128)} %copy.58) | data formatting | bytes 3145728 | tf_op jit(solution)/shard_map/reshape | solution.py:71
  211.3 4.3 %fusion.10 = (bf16[2,118,1536]{2,1,0:T(8,128)(2,1)S(1)}, f32[2,118,1536]{2,1,0:T(8,128)S(1)}, f32[2,118,1536]{2,1,0:T(8,128)S(1)}, f32[2,118,1536]{2,1,0:T(8,128)S(1)}) fusion(f32[2,118,1536]{2,0,1:T(2,128)} %param.16, f32[2,128,1536]{2,1,0:T(8,128)} %reshape.72, f32[]{:T(128)S(6)} %min.3, f32[2,118,1536]{2,0,1:T(2,128)} %param.19, f32[2,118,1536]{2,0,1:T(2,128)} %param.22), kind=kLoop, calls=%fused_computation.44 | loop fusion | flops 6162432 | bytes 10874884 | tf_op jit(solution)/shard_map/convert_element_type | solution.py:163
  215.8 3.2 %collective-permute-start.8 = (bf16[1,118,1536]{2,1,0:T(8,128)(2,1)S(1)}, bf16[1,118,1536]{2,1,0:T(8,128)(2,1)S(1)}, u32[]{:S(2)}, u32[]{:S(2)}) collective-permute-start(bf16[1,118,1536]{2,1,0:T(8,128)(2,1)S(1)} %get-tuple-element.84), channel_id=1, source_target_pairs={{0,5},{1,0},{4,1},{5,4},{2,7},{3,2},{6,3},{7,6},{8,13},{9,8},{12,9... | collective-permute-start | bytes 1087496 | tf_op jit(solution)/shard_map/ppermute | solution.py:78
  219.0 3.0 %fusion.13 = (bf16[2,1536,128]{2,1,0:T(8,128)(2,1)S(1)}, f32[2,1536,128]{2,1,0:T(8,128)}, f32[2,1536,128]{2,1,0:T(8,128)}, f32[2,1536,128]{2,1,0:T(8,128)}) fusion(f32[2,1536,128]{2,1,0:T(8,128)S(1)} %copy-done.3, f32[2,1536,128]{2,1,0:T(8,128)S(1)} %copy-done.4, f32[2,1536,128]{2,1,0:T(8,128)S(1)} %copy-done.5, f32[2,1536,128]{2,1,0:T(8,128)S(1)} %bitcast.68), kind=kLoop, calls=%fused_computation.45 | loop fusion | flops 6291456 | bytes 11796480 | tf_op jit(solution)/shard_map/convert_element_type | solution.py:162
  222.0 0.3 collective-permute-start.5
  222.4 2.2 copy.63
  224.6 2.2 copy.64
  226.8 2.2 copy.65
  229.1 4.1 %collective-permute-done.7 = bf16[1,118,1536]{2,1,0:T(8,128)(2,1)S(1)} collective-permute-done((bf16[1,118,1536]{2,1,0:T(8,128)(2,1)S(1)}, bf16[1,118,1536]{2,1,0:T(8,128)(2,1)S(1)}, u32[]{:S(2)}, u32[]{:S(2)}) %collective-permute-start.7) | collective-permute-done | bytes 362528 | tf_op jit(solution)/shard_map/ppermute | solution.py:77
  233.2 0.1 broadcast_select_fusion.5
  233.3 0.2 pad_maximum_fusion.3
  233.5 2.6 %copy.66 = bf16[2,118,3072]{2,0,1:T(2,128)(2,1)} copy(bf16[2,118,3072]{2,1,0:T(8,128)(2,1)S(1)} %pad_maximum_fusion.3) | data formatting | bytes 2899968
  236.1 4.7 %collective-permute-done.5 = bf16[1,1536,128]{2,1,0:T(8,128)(2,1)S(1)} collective-permute-done((bf16[1,1536,128]{2,1,0:T(8,128)(2,1)S(1)}, bf16[1,1536,128]{2,1,0:T(8,128)(2,1)S(1)}, u32[]{:S(2)}, u32[]{:S(2)}) %collective-permute-start.5) | collective-permute-done | bytes 393248 | tf_op jit(solution)/shard_map/ppermute | solution.py:77
  240.8 1.9 collective-permute-done.6
  242.7 0.2 broadcast_select_fusion.3
  242.9 1.2 pad_maximum_fusion.2
  244.2 1.2 constant_dynamic-update-slice_fusion.5
  245.4 1.2 constant_dynamic-update-slice_fusion.4
  246.6 0.4 broadcast_select_fusion.1
  247.0 1.9 pad_maximum_fusion.1
  (28 shorter events, 0.5 us)
Async XLA Ops:
  7.2 86.9 %reduce-scatter.3.cloned.1.call-start = ((), (), s32[]{:S(2)}) async-start(), calls=%async_computation.2 | async-start | bytes 3932160 | tf_op jit(solution)/shard_map/reduce_scatter | solution.py:37
  21.8 20.9 %collective-permute-start = (bf16[4,4,48,16,128]{4,3,2,1,0:T(8,128)(2,1)}, bf16[4,4,48,16,128]{4,3,2,1,0:T(8,128)(2,1)}, u32[]{:S(2)}, u32[]{:S(2)}) collective-permute-start(bf16[4,4,48,16,128]{4,3,2,1,0:T(8,128)(2,1)} %bitcast.8), channel_id=1, source_target_pairs={{2,0},{3,1},{6,4},{7,5},{10,8},{11,9},{14,12},{15,13},{18,16},{19,... | collective-permute-start | bytes 9437192 | tf_op jit(solution)/shard_map/ppermute | solution.py:31
  36.6 9.9 %collective-permute-start.1 = (bf16[4,4,48,16,128]{4,3,2,1,0:T(8,128)(2,1)S(1)}, bf16[4,4,48,16,128]{4,3,2,1,0:T(8,128)(2,1)}, u32[]{:S(2)}, u32[]{:S(2)}) collective-permute-start(bf16[4,4,48,16,128]{4,3,2,1,0:T(8,128)(2,1)S(1)} %bitcast.61), channel_id=1, source_target_pairs={{0,2},{1,3},{4,6},{5,7},{8,10},{9,11},{12,14},{13,15},{16,18},{17,... | collective-permute-start | bytes 9437192 | tf_op jit(solution)/shard_map/ppermute | solution.py:32
  53.2 65.6 %reduce-scatter.5.cloned.1.call-start = ((), (), s32[]{:S(2)}) async-start(), calls=%async_computation.3 | async-start | bytes 983040 | tf_op jit(solution)/shard_map/reduce_scatter | solution.py:38
  94.1 92.8 %all-gather.4.cloned.1.call-start = ((), (), s32[]{:S(2)}) async-start(), calls=%async_computation.4 | async-start | bytes 2359296 | tf_op jit(solution)/shard_map/all_gather | solution.py:51
  119.8 9.8 %collective-permute-start.2 = (f32[48,16,128]{2,1,0:T(8,128)S(1)}, f32[48,16,128]{2,1,0:T(8,128)S(1)}, u32[]{:S(2)}, u32[]{:S(2)}) collective-permute-start(f32[48,16,128]{2,1,0:T(8,128)S(1)} %bitcast_convert_fusion), channel_id=1, source_target_pairs={{0,32},{32,0},{64,96},{96,64},{1,33},{33,1},{65,97},{97,65},{2,34}... | collective-permute-start | bytes 1179656 | tf_op jit(solution)/shard_map/ppermute | solution.py:43
  130.6 10.4 %collective-permute-start.3 = (f32[48,16,128]{2,1,0:T(8,128)S(1)}, f32[48,16,128]{2,1,0:T(8,128)S(1)}, u32[]{:S(2)}, u32[]{:S(2)}) collective-permute-start(f32[48,16,128]{2,1,0:T(8,128)S(1)} %fusion.6), channel_id=1, source_target_pairs={{0,64},{32,96},{64,0},{96,32},{1,65},{33,97},{65,1},{97,33},{2,66}... | collective-permute-start | bytes 1179656 | tf_op jit(solution)/shard_map/ppermute | solution.py:43
  186.9 3.6 %collective-permute-start.4 = (bf16[2,4,48,16,128]{4,3,2,1,0:T(8,128)(2,1)}, bf16[2,4,48,16,128]{4,3,2,1,0:T(8,128)(2,1)S(1)}, u32[]{:S(2)}, u32[]{:S(2)}) collective-permute-start(bf16[2,4,48,16,128]{4,3,2,1,0:T(8,128)(2,1)} %bitcast.70), channel_id=1, source_target_pairs={{0,2},{2,0},{1,3},{3,1},{4,6},{6,4},{5,7},{7,5},{8,10},{10,8},{9,1... | collective-permute-start | bytes 4718600 | tf_op jit(solution)/shard_map/ppermute | solution.py:53
  192.8 1.9 copy-start.2
  193.0 2.7 %copy-start = (f32[512,1536]{1,0:T(8,128)S(1)}, f32[512,1536]{1,0:T(8,128)}, u32[]{:S(2)}) copy-start(f32[512,1536]{1,0:T(8,128)} %param.17) | copy-start | bytes 9437188
  193.0 3.6 %copy-start.1 = (f32[512,1536]{1,0:T(8,128)S(1)}, f32[512,1536]{1,0:T(8,128)}, u32[]{:S(2)}) copy-start(f32[512,1536]{1,0:T(8,128)} %param.20) | copy-start | bytes 9437188
  203.4 40.7 %collective-permute-start.9 = (bf16[256,1536]{1,0:T(8,128)(2,1)}, bf16[256,1536]{1,0:T(8,128)(2,1)}, u32[]{:S(2)}, u32[]{:S(2)}) collective-permute-start(bf16[256,1536]{1,0:T(8,128)(2,1)} %get-tuple-element.77), channel_id=1, source_target_pairs={{0,1},{1,4},{4,5},{5,0},{2,3},{3,6},{6,7},{7,2},{8,9},{9,12},{12,1... | collective-permute-start | bytes 2359304 | tf_op jit(solution)/shard_map/ppermute | solution.py:77
  204.0 41.4 %collective-permute-start.10 = (bf16[256,1536]{1,0:T(8,128)(2,1)}, bf16[256,1536]{1,0:T(8,128)(2,1)}, u32[]{:S(2)}, u32[]{:S(2)}) collective-permute-start(bf16[256,1536]{1,0:T(8,128)(2,1)} %get-tuple-element.76), channel_id=1, source_target_pairs={{0,5},{1,0},{4,1},{5,4},{2,7},{3,2},{6,3},{7,6},{8,13},{9,8},{12,9... | collective-permute-start | bytes 2359304 | tf_op jit(solution)/shard_map/ppermute | solution.py:78
  211.3 7.7 %copy-start.3 = (f32[2,1536,128]{2,1,0:T(8,128)S(1)}, f32[2,1536,128]{2,1,0:T(8,128)}, u32[]{:S(2)}) copy-start(f32[2,1536,128]{2,1,0:T(8,128)} %param.15) | copy-start | bytes 4718596
  211.3 7.7 %copy-start.4 = (f32[2,1536,128]{2,1,0:T(8,128)S(1)}, f32[2,1536,128]{2,1,0:T(8,128)}, u32[]{:S(2)}) copy-start(f32[2,1536,128]{2,1,0:T(8,128)} %param.18) | copy-start | bytes 4718596
  211.3 7.7 %copy-start.5 = (f32[2,1536,128]{2,1,0:T(8,128)S(1)}, f32[2,1536,128]{2,1,0:T(8,128)}, u32[]{:S(2)}) copy-start(f32[2,1536,128]{2,1,0:T(8,128)} %param.21) | copy-start | bytes 4718596
  215.7 17.5 %collective-permute-start.7 = (bf16[1,118,1536]{2,1,0:T(8,128)(2,1)S(1)}, bf16[1,118,1536]{2,1,0:T(8,128)(2,1)S(1)}, u32[]{:S(2)}, u32[]{:S(2)}) collective-permute-start(bf16[1,118,1536]{2,1,0:T(8,128)(2,1)S(1)} %get-tuple-element.85), channel_id=1, source_target_pairs={{0,1},{1,4},{4,5},{5,0},{2,3},{3,6},{6,7},{7,2},{8,9},{9,12},{12,1... | collective-permute-start | bytes 1087496 | tf_op jit(solution)/shard_map/ppermute | solution.py:77
  215.8 17.4 %collective-permute-start.8 = (bf16[1,118,1536]{2,1,0:T(8,128)(2,1)S(1)}, bf16[1,118,1536]{2,1,0:T(8,128)(2,1)S(1)}, u32[]{:S(2)}, u32[]{:S(2)}) collective-permute-start(bf16[1,118,1536]{2,1,0:T(8,128)(2,1)S(1)} %get-tuple-element.84), channel_id=1, source_target_pairs={{0,5},{1,0},{4,1},{5,4},{2,7},{3,2},{6,3},{7,6},{8,13},{9,8},{12,9... | collective-permute-start | bytes 1087496 | tf_op jit(solution)/shard_map/ppermute | solution.py:78
  222.0 18.7 %collective-permute-start.5 = (bf16[1,1536,128]{2,1,0:T(8,128)(2,1)S(1)}, bf16[1,1536,128]{2,1,0:T(8,128)(2,1)S(1)}, u32[]{:S(2)}, u32[]{:S(2)}) collective-permute-start(bf16[1,1536,128]{2,1,0:T(8,128)(2,1)S(1)} %get-tuple-element.83), channel_id=1, source_target_pairs={{0,1},{1,4},{4,5},{5,0},{2,3},{3,6},{6,7},{7,2},{8,9},{9,12},{12,1... | collective-permute-start | bytes 1179656 | tf_op jit(solution)/shard_map/ppermute | solution.py:77
  233.1 9.5 %collective-permute-start.6 = (bf16[1,1536,128]{2,1,0:T(8,128)(2,1)S(1)}, bf16[1,1536,128]{2,1,0:T(8,128)(2,1)S(1)}, u32[]{:S(2)}, u32[]{:S(2)}) collective-permute-start(bf16[1,1536,128]{2,1,0:T(8,128)(2,1)S(1)} %get-tuple-element.82), channel_id=1, source_target_pairs={{0,5},{1,0},{4,1},{5,4},{2,7},{3,2},{6,3},{7,6},{8,13},{9,8},{12,9... | collective-permute-start | bytes 1179656 | tf_op jit(solution)/shard_map/ppermute | solution.py:78
Sparse Core Ops, SparseCore 0:
  53.4 40.6 reduce-scatter.2
  96.5 22.2 reduce-scatter.4
  155.9 31.0 all-gather.3

commit v2 on v0

--- a/solution.py
+++ b/solution.py
@@ -74,10 +74,13 @@
 
 
 def place(own, other, axis):
-    low = lax.axis_index("shard") == 0
-    lo = jnp.where(low, own, other)
-    hi = jnp.where(low, other, own)
-    return jnp.concatenate([lo, hi], axis=axis)
+    s = lax.axis_index("shard")
+    size = own.shape[axis]
+    shape = list(own.shape)
+    shape[axis] = 2 * size
+    full = jnp.zeros(shape, own.dtype)
+    full = lax.dynamic_update_slice_in_dim(full, other, (1 - s) * size, axis)
+    return lax.dynamic_update_slice_in_dim(full, own, s * size, axis)
 
 
 def on_device(

time: 256 us -> 254 us (level)
    concatenate x3 -> x1, other arithmetic: 3.29 us -> 0.07 us  [swap_halves(): return jnp.concatenate([from_left, from_right], axis=split_axis)]
    unnamed x19 -> x21, local copies, waits for them, and re-layouts: 12.8 us -> 11.5 us
  transfers between devices with their start and end apart: 12 -> 12, of which waited for: 8 -> 8; matrix products, arithmetic and copies ran while one was open for 15% -> 14% of each run, Pallas kernels for 0% -> 0%
where the time goes in v2:
time: 254 us
  waiting for transfers between devices  89.5 us (35%)
  blocking collectives  59.1 us (23%)
  other arithmetic  43.1 us (17%)
  local copies, waits for them, and re-layouts  31.6 us (12%)
  between operations  15.9 us (6%)
  starting transfers between devices  14.6 us (6%)
    reduce_scatter x1, waiting for transfers between devices, reduce_flat(): part = lax.psum_scatter(part, XRING, scatter_dimension=0, tiled=False)  40.8 us
    reduce_scatter x1, waiting for transfers between devices, reduce_flat(): part = lax.psum_scatter(part, 'y', scatter_dimension=0, tiled=False)  24.6 us
    psum x3, blocking collectives, reduce_flat(): squares = lax.psum(squares, axis)  22.9 us
    psum x1, blocking collectives, reduce_flat(): part = lax.psum(part.astype(jnp.float32), 'z').astype(jnp.bfloat16)  21 us
    all_gather x1, blocking collectives, reduce_flat(): part = lax.all_gather(part, 'y', axis=0)  15.1 us
    unnamed x21, local copies, waits for them, and re-layouts  11.5 us
    ppermute x3, waiting for transfers between devices, swap_halves(): lax.ppermute(first, XRING, perm=[(p, (p + 1) % n) for p in range(n)])  9.62 us
    convert_element_type x1, other arithmetic, reduce_flat(): (mine.astype(jnp.float32) + got.astype(jnp.float32)).astype(jnp.bfloat16)  6.71 us
  transfers between devices with their start and end apart: 12, of which 8 were waited for; matrix products, arithmetic and copies ran while one was open for 14% of the time, Pallas kernels for 0%

profile of v2, /device:TPU:0, one launch (start us, length us, event | category | flops | bytes accessed | tf_op | source)
XLA Modules:
  0.0 253.9 jit_solution(12126340490341801501)
XLA Ops:
  7.2 6.5 %reduce = bf16[2,118,3072]{2,0,1:T(2,128)(2,1)S(1)} reduce(bf16[2,2,118,3072]{3,1,2,0:T(2,128)(2,1)} %param.13, bf16[]{:T(256)} %constant.26.clone.1), dimensions={0}, to_apply=%region_0.0.clone | reduce | flops 724992 | bytes 4349954 | tf_op jit(solution)/shard_map/reduce_sum | solution.py:117
  13.7 1.2 pad.5
  14.9 1.0 reshape.77
  16.0 0.4 copy.54
  16.4 0.3 copy.55
  16.7 2.9 %reduce.1 = bf16[2,3072,128]{2,1,0:T(8,128)(2,1)S(1)} reduce(bf16[2,2,3072,128]{3,2,1,0:T(8,128)(2,1)} %param.12, bf16[]{:T(256)} %constant.26.clone.1), dimensions={0}, to_apply=%region_1.0.clone | reduce | flops 786432 | bytes 4718594 | tf_op jit(solution)/shard_map/reduce_sum | solution.py:112
  19.6 0.3 copy.56
  19.9 1.9 pad_maximum_fusion
  21.8 1.5 collective-permute-start
  23.3 6.1 %reduce.2 = bf16[1024,1536]{1,0:T(8,128)(2,1)S(1)} reduce(bf16[2,1024,1536]{2,1,0:T(8,128)(2,1)} %param.14, bf16[]{:T(256)} %constant.26.clone.1), dimensions={0}, to_apply=%region_2.3.clone | reduce | flops 1572864 | bytes 9437186 | tf_op jit(solution)/shard_map/reduce_sum | solution.py:123
  29.4 3.7 %reshape.70 = bf16[64,16,12,128]{3,2,1,0:T(8,128)(2,1)} reshape(bf16[1024,1536]{1,0:T(8,128)(2,1)S(1)} %reduce.2) | data formatting | bytes 6291456 | tf_op jit(solution)/shard_map/reshape | solution.py:57
  33.0 3.0 %copy.57 = bf16[64,12,16,128]{3,2,1,0:T(8,128)(2,1)S(1)} copy(bf16[64,12,16,128]{3,1,2,0:T(8,128)(2,1)} %bitcast.55) | data formatting | bytes 6291456 | tf_op jit(solution)/shard_map/convert_element_type | solution.py:30
  36.0 0.5 copy.58
  36.6 6.2 %collective-permute-start.1 = (bf16[4,4,48,16,128]{4,3,2,1,0:T(8,128)(2,1)S(1)}, bf16[4,4,48,16,128]{4,3,2,1,0:T(8,128)(2,1)}, u32[]{:S(2)}, u32[]{:S(2)}) collective-permute-start(bf16[4,4,48,16,128]{4,3,2,1,0:T(8,128)(2,1)S(1)} %bitcast.59), channel_id=1, source_target_pairs={{0,2},{1,3},{4,6},{5,7},{8,10},{9,11},{12,14},{13,15},{16,18},{17,... | collective-permute-start | bytes 9437192 | tf_op jit(solution)/shard_map/ppermute | solution.py:32
  42.8 3.7 %collective-permute-done.1 = bf16[4,4,48,16,128]{4,3,2,1,0:T(8,128)(2,1)} collective-permute-done((bf16[4,4,48,16,128]{4,3,2,1,0:T(8,128)(2,1)S(1)}, bf16[4,4,48,16,128]{4,3,2,1,0:T(8,128)(2,1)}, u32[]{:S(2)}, u32[]{:S(2)}) %collective-permute-start.1) | collective-permute-done | bytes 3145760 | tf_op jit(solution)/shard_map/ppermute | solution.py:32
  46.5 6.7 %add_convert_fusion = bf16[4,4,48,16,128]{4,3,2,1,0:T(8,128)(2,1)} fusion(bf16[4,4,48,16,128]{4,3,2,1,0:T(8,128)(2,1)} %collective-permute-done, bf16[4,4,48,16,128]{4,3,2,1,0:T(8,128)(2,1)} %collective-permute-done.1, pred[]{:T(512)S(6)} %eq.3, bf16[2,2,4,48,16,128]{5,4,3,2,1,0:T(8,128)(2,1)S(1)} %copy.58, bf16[2,2,4,48,16,128]{5,4,3,2,1,0:T(8,128)(2,1)} %pad_maximum_fusion), kind=kLoop, calls=%fused_computation.1 | loop fusion | flops 9437184 | bytes 15728641 | tf_op jit(solution)/shard_map/convert_element_type | solution.py:36
  53.3 40.8 %reduce-scatter.3.cloned.1.call-done = bf16[1,4,48,16,128]{4,3,2,1,0:T(8,128)(2,1)} async-done(((bf16[4,4,48,16,128]{4,3,2,1,0:T(8,128)(2,1)}), bf16[1,4,48,16,128]{4,3,2,1,0:T(8,128)(2,1)}) %reduce-scatter.3.cloned.1.call-update) | async-done | bytes 786448 | tf_op jit(solution)/shard_map/reduce_scatter | solution.py:37
  94.2 24.6 %reduce-scatter.5.cloned.1.call-done = bf16[1,48,16,128]{3,2,1,0:T(8,128)(2,1)} async-done(((bf16[4,48,16,128]{3,2,1,0:T(8,128)(2,1)}), bf16[1,48,16,128]{3,2,1,0:T(8,128)(2,1)}) %reduce-scatter.5.cloned.1.call-update) | async-done | bytes 196624 | tf_op jit(solution)/shard_map/reduce_scatter | solution.py:38
  118.8 1.0 bitcast_convert_fusion
  119.8 21.0 %all-reduce.2 = bf16[48,16,128]{2,1,0:T(8,128)(2,1)S(1)} all-reduce(f32[48,16,128]{2,1,0:T(8,128)S(1)} %bitcast_convert_fusion), channel_id=1, replica_groups=mesh['z'=4,'y'=4,'xh'=2,'core'=2,'shard'=2] {'z'}, use_global_device_ids=true, to_apply=%region_5.6 | all-reduce | flops 98304 | bytes 589824 | tf_op jit(solution)/shard_map/psum | solution.py:39
  140.8 15.1 %all-gather = bf16[192,16,128]{2,1,0:T(8,128)(2,1)} all-gather(bf16[48,16,128]{2,1,0:T(8,128)(2,1)S(1)} %all-reduce.2), channel_id=2, replica_groups=mesh['z'=4,'y'=4,'xh'=2,'core'=2,'shard'=2] {'y'}, dimensions={0}, use_global_device_ids=true | all-gather | bytes 983040 | tf_op jit(solution)/shard_map/all_gather | solution.py:44
  155.9 0.7 multiply_reduce_fusion
  156.6 3.1 %psum.29 = f32[]{:T(128)} all-reduce(f32[]{:T(128)} %multiply_reduce_fusion), channel_id=1, replica_groups=mesh['z'=4,'y'=4,'xh'=2,'core'=2,'shard'=2] {'core'}, use_global_device_ids=true, to_apply=%region_7.8 | all-reduce | flops 1 | bytes 8 | tf_op jit(solution)/shard_map/psum | solution.py:43
  159.7 11.4 %psum.30 = f32[]{:T(128)} all-reduce(f32[]{:T(128)} %psum.29), channel_id=1, replica_groups=mesh['z'=4,'y'=4,'xh'=2,'core'=2,'shard'=2] {'xh','shard'}, use_global_device_ids=true, to_apply=%region_8.9 | all-reduce | flops 1 | bytes 8 | tf_op jit(solution)/shard_map/psum | solution.py:43
  171.1 8.5 %psum.31 = f32[]{:T(128)} all-reduce(f32[]{:T(128)} %psum.30), channel_id=1, replica_groups=mesh['z'=4,'y'=4,'xh'=2,'core'=2,'shard'=2] {'y'}, use_global_device_ids=true, to_apply=%region_9.10 | all-reduce | flops 1 | bytes 8 | tf_op jit(solution)/shard_map/psum | solution.py:43
  179.6 5.9 %all-gather.4.cloned.1.call-done = bf16[8,48,16,128]{3,2,1,0:T(8,128)(2,1)} async-done(((bf16[4,48,16,128]{3,2,1,0:T(8,128)(2,1)}), bf16[8,48,16,128]{3,2,1,0:T(8,128)(2,1)}) %all-gather.4.cloned.1.call-update) | async-done | bytes 1572880 | tf_op jit(solution)/shard_map/all_gather | solution.py:45
  186.2 2.9 %collective-permute-done.2 = bf16[2,4,48,16,128]{4,3,2,1,0:T(8,128)(2,1)S(1)} collective-permute-done((bf16[2,4,48,16,128]{4,3,2,1,0:T(8,128)(2,1)}, bf16[2,4,48,16,128]{4,3,2,1,0:T(8,128)(2,1)S(1)}, u32[]{:S(2)}, u32[]{:S(2)}) %collective-permute-start.2) | collective-permute-done | bytes 1572896 | tf_op jit(solution)/shard_map/ppermute | solution.py:47
  189.1 1.6 select_bitcast_fusion.1
  190.7 0.6 convert_multiply_fusion
  191.3 0.2 slice_multiply_fusion
  191.6 1.3 copy.64
  192.9 0.3 copy-done.2
  193.2 1.0 copy-done
  194.2 0.9 copy-done.1
  195.2 5.6 %fusion.6 = (bf16[512,1536]{1,0:T(8,128)(2,1)S(1)}, f32[512,1536]{1,0:T(8,128)}, f32[512,1536]{1,0:T(8,128)}, f32[512,1536]{1,0:T(8,128)}) fusion(f32[512,1536]{1,0:T(8,128)S(1)} %copy-done, f32[64,8,12,128]{3,2,1,0:T(8,128)S(1)} %bitcast.56, f32[512,1536]{1,0:T(8,128)S(1)} %copy-done.1, f32[512,1536]{1,0:T(8,128)S(1)} %copy-done.2), kind=kLoop, calls=%fused_computation.33 | loop fusion | flops 12582912 | bytes 23592960 | tf_op jit(solution)/shard_map/convert_element_type | solution.py:161
  200.7 1.3 fusion.16
  202.0 0.5 collective-permute-start.7
  202.5 2.8 %collective-permute-start.8 = (bf16[256,1536]{1,0:T(8,128)(2,1)}, bf16[256,1536]{1,0:T(8,128)(2,1)}, u32[]{:S(2)}, u32[]{:S(2)}) collective-permute-start(bf16[256,1536]{1,0:T(8,128)(2,1)} %get-tuple-element.73), channel_id=1, source_target_pairs={{0,5},{1,0},{4,1},{5,4},{2,7},{3,2},{6,3},{7,6},{8,13},{9,8},{12,9... | collective-permute-start | bytes 2359304 | tf_op jit(solution)/shard_map/ppermute | solution.py:72
  205.2 0.2 fusion.15
  205.4 1.8 copy.60
  207.3 2.6 %reshape.72 = f32[2,128,1536]{2,1,0:T(8,128)} reshape(f32[2,8,16,12,128]{4,3,2,1,0:T(8,128)} %copy.60) | data formatting | bytes 3145728 | tf_op jit(solution)/shard_map/reshape | solution.py:65
  209.9 4.3 %fusion.9 = (bf16[2,118,1536]{2,1,0:T(8,128)(2,1)S(1)}, f32[2,118,1536]{2,1,0:T(8,128)S(1)}, f32[2,118,1536]{2,1,0:T(8,128)S(1)}, f32[2,118,1536]{2,1,0:T(8,128)S(1)}) fusion(f32[2,118,1536]{2,0,1:T(2,128)} %param.16, f32[2,128,1536]{2,1,0:T(8,128)} %reshape.72, f32[]{:T(128)S(6)} %min.3, f32[2,118,1536]{2,0,1:T(2,128)} %param.19, f32[2,118,1536]{2,0,1:T(2,128)} %param.22), kind=kLoop, calls=%fused_computation.34 | loop fusion | flops 6162432 | bytes 10874884 | tf_op jit(solution)/shard_map/convert_element_type | solution.py:160
  214.2 0.1 collective-permute-start.5
  214.3 3.2 %collective-permute-start.6 = (bf16[1,118,1536]{2,1,0:T(8,128)(2,1)S(1)}, bf16[1,118,1536]{2,1,0:T(8,128)(2,1)S(1)}, u32[]{:S(2)}, u32[]{:S(2)}) collective-permute-start(bf16[1,118,1536]{2,1,0:T(8,128)(2,1)S(1)} %get-tuple-element.77), channel_id=1, source_target_pairs={{0,5},{1,0},{4,1},{5,4},{2,7},{3,2},{6,3},{7,6},{8,13},{9,8},{12,9... | collective-permute-start | bytes 1087496 | tf_op jit(solution)/shard_map/ppermute | solution.py:72
  217.5 3.0 %fusion.12 = (bf16[2,1536,128]{2,1,0:T(8,128)(2,1)S(1)}, f32[2,1536,128]{2,1,0:T(8,128)}, f32[2,1536,128]{2,1,0:T(8,128)}, f32[2,1536,128]{2,1,0:T(8,128)}) fusion(f32[2,1536,128]{2,1,0:T(8,128)S(1)} %copy-done.5, f32[2,1536,128]{2,1,0:T(8,128)S(1)} %copy-done.6, f32[2,1536,128]{2,1,0:T(8,128)S(1)} %copy-done.7, f32[2,1536,128]{2,1,0:T(8,128)S(1)} %bitcast.66), kind=kLoop, calls=%fused_computation.35 | loop fusion | flops 6291456 | bytes 11796480 | tf_op jit(solution)/shard_map/convert_element_type | solution.py:159
  220.6 0.3 collective-permute-start.3
  220.9 2.2 copy.67
  223.2 2.2 copy.68
  225.4 2.2 copy.69
  227.6 4.1 %collective-permute-done.5 = bf16[1,118,1536]{2,1,0:T(8,128)(2,1)S(1)} collective-permute-done((bf16[1,118,1536]{2,1,0:T(8,128)(2,1)S(1)}, bf16[1,118,1536]{2,1,0:T(8,128)(2,1)S(1)}, u32[]{:S(2)}, u32[]{:S(2)}) %collective-permute-start.5) | collective-permute-done | bytes 362528 | tf_op jit(solution)/shard_map/ppermute | solution.py:71
  231.7 0.1 pad_maximum_fusion.1
  231.8 0.7 broadcast_in_dim.10
  232.5 0.6 copy_dynamic-update-slice_fusion.1
  233.2 0.6 copy_dynamic-update-slice_fusion
  233.8 5.5 %collective-permute-done.3 = bf16[1,1536,128]{2,1,0:T(8,128)(2,1)S(1)} collective-permute-done((bf16[1,1536,128]{2,1,0:T(8,128)(2,1)S(1)}, bf16[1,1536,128]{2,1,0:T(8,128)(2,1)S(1)}, u32[]{:S(2)}, u32[]{:S(2)}) %collective-permute-start.3) | collective-permute-done | bytes 393248 | tf_op jit(solution)/shard_map/ppermute | solution.py:71
  239.3 1.9 collective-permute-done.4
  241.2 0.2 broadcast_in_dim.9
  241.4 0.1 maximum_dynamic-update-slice_fusion.1
  241.6 0.1 constant_dynamic-update-slice_fusion.1
  241.7 0.2 broadcast_in_dim.11
  241.9 0.9 copy-done.4
  242.8 1.5 maximum_dynamic-update-slice_fusion
  244.4 0.2 constant_dynamic-update-slice_fusion
  244.5 1.7 copy-done.3
  (27 shorter events, 0.3 us)
Async XLA Ops:
  7.2 86.9 %reduce-scatter.3.cloned.1.call-start = ((), (), s32[]{:S(2)}) async-start(), calls=%async_computation.2 | async-start | bytes 3932160 | tf_op jit(solution)/shard_map/reduce_scatter | solution.py:37
  21.8 20.9 %collective-permute-start = (bf16[4,4,48,16,128]{4,3,2,1,0:T(8,128)(2,1)}, bf16[4,4,48,16,128]{4,3,2,1,0:T(8,128)(2,1)}, u32[]{:S(2)}, u32[]{:S(2)}) collective-permute-start(bf16[4,4,48,16,128]{4,3,2,1,0:T(8,128)(2,1)} %bitcast.8), channel_id=1, source_target_pairs={{2,0},{3,1},{6,4},{7,5},{10,8},{11,9},{14,12},{15,13},{18,16},{19,... | collective-permute-start | bytes 9437192 | tf_op jit(solution)/shard_map/ppermute | solution.py:31
  36.6 9.9 %collective-permute-start.1 = (bf16[4,4,48,16,128]{4,3,2,1,0:T(8,128)(2,1)S(1)}, bf16[4,4,48,16,128]{4,3,2,1,0:T(8,128)(2,1)}, u32[]{:S(2)}, u32[]{:S(2)}) collective-permute-start(bf16[4,4,48,16,128]{4,3,2,1,0:T(8,128)(2,1)S(1)} %bitcast.59), channel_id=1, source_target_pairs={{0,2},{1,3},{4,6},{5,7},{8,10},{9,11},{12,14},{13,15},{16,18},{17,... | collective-permute-start | bytes 9437192 | tf_op jit(solution)/shard_map/ppermute | solution.py:32
  53.2 65.6 %reduce-scatter.5.cloned.1.call-start = ((), (), s32[]{:S(2)}) async-start(), calls=%async_computation.3 | async-start | bytes 983040 | tf_op jit(solution)/shard_map/reduce_scatter | solution.py:38
  94.1 91.3 %all-gather.4.cloned.1.call-start = ((), (), s32[]{:S(2)}) async-start(), calls=%async_computation.4 | async-start | bytes 2359296 | tf_op jit(solution)/shard_map/all_gather | solution.py:45
  185.5 3.6 %collective-permute-start.2 = (bf16[2,4,48,16,128]{4,3,2,1,0:T(8,128)(2,1)}, bf16[2,4,48,16,128]{4,3,2,1,0:T(8,128)(2,1)S(1)}, u32[]{:S(2)}, u32[]{:S(2)}) collective-permute-start(bf16[2,4,48,16,128]{4,3,2,1,0:T(8,128)(2,1)} %bitcast.68), channel_id=1, source_target_pairs={{0,2},{2,0},{1,3},{3,1},{4,6},{6,4},{5,7},{7,5},{8,10},{10,8},{9,1... | collective-permute-start | bytes 4718600 | tf_op jit(solution)/shard_map/ppermute | solution.py:47
  191.3 1.9 copy-start.2
  191.6 2.7 %copy-start = (f32[512,1536]{1,0:T(8,128)S(1)}, f32[512,1536]{1,0:T(8,128)}, u32[]{:S(2)}) copy-start(f32[512,1536]{1,0:T(8,128)} %param.17) | copy-start | bytes 9437188
  191.6 3.6 %copy-start.1 = (f32[512,1536]{1,0:T(8,128)S(1)}, f32[512,1536]{1,0:T(8,128)}, u32[]{:S(2)}) copy-start(f32[512,1536]{1,0:T(8,128)} %param.20) | copy-start | bytes 9437188
  202.0 39.7 %collective-permute-start.7 = (bf16[256,1536]{1,0:T(8,128)(2,1)}, bf16[256,1536]{1,0:T(8,128)(2,1)}, u32[]{:S(2)}, u32[]{:S(2)}) collective-permute-start(bf16[256,1536]{1,0:T(8,128)(2,1)} %get-tuple-element.72), channel_id=1, source_target_pairs={{0,1},{1,4},{4,5},{5,0},{2,3},{3,6},{6,7},{7,2},{8,9},{9,12},{12,1... | collective-permute-start | bytes 2359304 | tf_op jit(solution)/shard_map/ppermute | solution.py:71
  202.5 39.2 %collective-permute-start.8 = (bf16[256,1536]{1,0:T(8,128)(2,1)}, bf16[256,1536]{1,0:T(8,128)(2,1)}, u32[]{:S(2)}, u32[]{:S(2)}) collective-permute-start(bf16[256,1536]{1,0:T(8,128)(2,1)} %get-tuple-element.73), channel_id=1, source_target_pairs={{0,5},{1,0},{4,1},{5,4},{2,7},{3,2},{6,3},{7,6},{8,13},{9,8},{12,9... | collective-permute-start | bytes 2359304 | tf_op jit(solution)/shard_map/ppermute | solution.py:72
  209.9 7.7 %copy-start.5 = (f32[2,1536,128]{2,1,0:T(8,128)S(1)}, f32[2,1536,128]{2,1,0:T(8,128)}, u32[]{:S(2)}) copy-start(f32[2,1536,128]{2,1,0:T(8,128)} %param.15) | copy-start | bytes 4718596
  209.9 7.7 %copy-start.6 = (f32[2,1536,128]{2,1,0:T(8,128)S(1)}, f32[2,1536,128]{2,1,0:T(8,128)}, u32[]{:S(2)}) copy-start(f32[2,1536,128]{2,1,0:T(8,128)} %param.18) | copy-start | bytes 4718596
  209.9 7.7 %copy-start.7 = (f32[2,1536,128]{2,1,0:T(8,128)S(1)}, f32[2,1536,128]{2,1,0:T(8,128)}, u32[]{:S(2)}) copy-start(f32[2,1536,128]{2,1,0:T(8,128)} %param.21) | copy-start | bytes 4718596
  214.2 17.5 %collective-permute-start.5 = (bf16[1,118,1536]{2,1,0:T(8,128)(2,1)S(1)}, bf16[1,118,1536]{2,1,0:T(8,128)(2,1)S(1)}, u32[]{:S(2)}, u32[]{:S(2)}) collective-permute-start(bf16[1,118,1536]{2,1,0:T(8,128)(2,1)S(1)} %get-tuple-element.76), channel_id=1, source_target_pairs={{0,1},{1,4},{4,5},{5,0},{2,3},{3,6},{6,7},{7,2},{8,9},{9,12},{12,1... | collective-permute-start | bytes 1087496 | tf_op jit(solution)/shard_map/ppermute | solution.py:71
  214.3 17.4 %collective-permute-start.6 = (bf16[1,118,1536]{2,1,0:T(8,128)(2,1)S(1)}, bf16[1,118,1536]{2,1,0:T(8,128)(2,1)S(1)}, u32[]{:S(2)}, u32[]{:S(2)}) collective-permute-start(bf16[1,118,1536]{2,1,0:T(8,128)(2,1)S(1)} %get-tuple-element.77), channel_id=1, source_target_pairs={{0,5},{1,0},{4,1},{5,4},{2,7},{3,2},{6,3},{7,6},{8,13},{9,8},{12,9... | collective-permute-start | bytes 1087496 | tf_op jit(solution)/shard_map/ppermute | solution.py:72
  220.6 18.7 %collective-permute-start.3 = (bf16[1,1536,128]{2,1,0:T(8,128)(2,1)S(1)}, bf16[1,1536,128]{2,1,0:T(8,128)(2,1)S(1)}, u32[]{:S(2)}, u32[]{:S(2)}) collective-permute-start(bf16[1,1536,128]{2,1,0:T(8,128)(2,1)S(1)} %get-tuple-element.74), channel_id=1, source_target_pairs={{0,1},{1,4},{4,5},{5,0},{2,3},{3,6},{6,7},{7,2},{8,9},{9,12},{12,1... | collective-permute-start | bytes 1179656 | tf_op jit(solution)/shard_map/ppermute | solution.py:71
  231.7 9.5 %collective-permute-start.4 = (bf16[1,1536,128]{2,1,0:T(8,128)(2,1)S(1)}, bf16[1,1536,128]{2,1,0:T(8,128)(2,1)S(1)}, u32[]{:S(2)}, u32[]{:S(2)}) collective-permute-start(bf16[1,1536,128]{2,1,0:T(8,128)(2,1)S(1)} %get-tuple-element.75), channel_id=1, source_target_pairs={{0,5},{1,0},{4,1},{5,4},{2,7},{3,2},{6,3},{7,6},{8,13},{9,8},{12,9... | collective-permute-start | bytes 1179656 | tf_op jit(solution)/shard_map/ppermute | solution.py:72
  233.8 7.8 %copy-start.8 = (bf16[2,118,3072]{2,0,1:T(2,128)(2,1)}, bf16[2,118,3072]{2,0,1:T(2,128)(2,1)S(1)}, u32[]{:S(2)}) copy-start(bf16[2,118,3072]{2,0,1:T(2,128)(2,1)S(1)} %copy_dynamic-update-slice_fusion) | copy-start | bytes 4349956
  241.7 1.1 copy-start.4
  244.5 1.7 copy-start.3
Sparse Core Ops, SparseCore 0:
  53.4 40.6 reduce-scatter.2
  96.5 22.2 reduce-scatter.4
  156.1 29.3 all-gather.3
